TPU v7x, 128 devices: a whole 4x4x4 slice. The times are simulated.
128 devices in a mesh: ctx: 16 (over x, y_hi, core), head: 8 (over z, y_lo).
Axes of the slice: x: 4, y: 4 (y_hi: 2, y_lo: 2; y = y_hi * 2 + y_lo), z: 4, core: 2. Of those that a mesh axis runs over, the one named last changes fastest.
Arguments:
- activations: bfloat16 [8192, 4096], P('ctx')
- qkv_weight: bfloat16 [4096, 3, 32, 128], P(None, None, 'head'), may hold values from -0.09375 to 0.09375
- out_weight: bfloat16 [32, 128, 4096], P('head'), may hold values from -0.09375 to 0.09375
- mod_table: float32 [16, 4096], replicated, may hold values from -3 to 3
- clip_level: int32 [64], replicated, may hold values from 0 to 15
- clip_of: int32 [8192], P('ctx'), may hold values from 0 to 63, never falling along the last dimension, each value on 1 to 256 neighbouring positions
- visible: int32 [64, 64], replicated, may hold values from 0 to 1, as said below
Outputs:
- mixed: bfloat16 [8192, 4096], P(('ctx', 'head'))
Inputs may be any that keep to these rules, and one draw needn't show every extreme that they name: visible is 1 on the diagonal and 0 above it. `clip_of`: clip numbers never fall along the tokens; every clip has 1 to 256 tokens and one has exactly 256.
All inputs are finite; a program needn't handle non-finite values.
Results may differ from a plain program's by a relative error of at most 0.02.
The roundings to bfloat16 on the way count: a program that leaves them out, or rounds other values in their place, can miss the bound.
Values may be sent and summed in bfloat16 or wider, within the bound.
No kernel may reach another device: no remote copies, remote signals or barrier semaphores. Data moves between devices by JAX's collectives and lax.ppermute only.
A program may use at most 128 MiB of HBM per device.

v0:
```python
import math
import jax
import jax.numpy as jnp
from jax import lax
from jax.sharding import PartitionSpec as P


def score_block(state_now, kv_block, key_clips, queries, query_vis, score_scale):
    clip_count = query_vis.shape[1]
    clip_ids = lax.broadcasted_iota(jnp.int32, (1, clip_count), 1)
    key_hot = (key_clips[:, None] == clip_ids).astype(jnp.float32)
    allowed = jnp.dot(query_vis, key_hot.T, precision=lax.Precision.HIGHEST) > 0.5
    top_score, totals, summed = state_now
    key_rows = kv_block[:, 0]
    value_rows = kv_block[:, 1]
    scores = (
        jnp.einsum("rhd,khd->hrk", queries, key_rows, preferred_element_type=jnp.float32)
        * score_scale
    )
    masked = jnp.where(allowed[None], scores, -1e30)
    new_top = jnp.maximum(top_score, jnp.max(masked, axis=2))
    weights = jnp.where(allowed[None], jnp.exp(masked - new_top[:, :, None]), 0.0)
    factor = jnp.exp(top_score - new_top)
    totals = totals * factor + jnp.sum(weights, axis=2)
    summed = summed * factor[:, :, None] + jnp.einsum(
        "hrk,khd->hrd", weights.astype(jnp.bfloat16), value_rows, preferred_element_type=jnp.float32
    )
    return (new_top, totals, summed)


def fold_keys(state_now, kv_rows, key_clips, queries, query_vis, score_scale):
    key_count = kv_rows.shape[0]
    block_rows = math.gcd(key_count, 512)

    def one_block(block_index, state_in):
        first_row = block_index * block_rows
        kv_block = lax.dynamic_slice_in_dim(kv_rows, first_row, block_rows, 0)
        clip_block = lax.dynamic_slice_in_dim(key_clips, first_row, block_rows, 0)
        return score_block(state_in, kv_block, clip_block, queries, query_vis, score_scale)

    return lax.fori_loop(0, key_count // block_rows, one_block, state_now)


def per_device(activations, qkv_weight, out_weight, mod_table, clip_level, clip_of, visible):
    heads_here = qkv_weight.shape[2]
    head_size = qkv_weight.shape[3]
    clip_count = visible.shape[0]
    level_count = mod_table.shape[0]
    clip_ids = lax.broadcasted_iota(jnp.int32, (1, clip_count), 1)
    level_ids = lax.broadcasted_iota(jnp.int32, (1, level_count), 1)
    tok_hot = clip_of[:, None] == clip_ids
    level_rows = jnp.sum(jnp.where(tok_hot, clip_level[None, :], 0), axis=1)
    level_hot = (level_rows[:, None] == level_ids).astype(jnp.float32)
    modulation = jnp.dot(level_hot, mod_table, precision=lax.Precision.HIGHEST)
    moduled = (activations.astype(jnp.float32) * (1.0 + modulation)).astype(jnp.bfloat16)
    qkv = jnp.einsum(
        "td,dchk->tchk", moduled, qkv_weight, preferred_element_type=jnp.float32
    ).astype(jnp.bfloat16)
    queries = qkv[:, 0]
    kv_local = qkv[:, 1:3]
    query_count = queries.shape[0]
    query_hot = (clip_of[:, None] == clip_ids).astype(jnp.float32)
    query_vis = jnp.dot(query_hot, visible.astype(jnp.float32), precision=lax.Precision.HIGHEST)
    score_scale = 1.0 / jnp.sqrt(jnp.float32(head_size))
    initial = (
        jnp.full((heads_here, query_count), -1e30, jnp.float32),
        jnp.zeros((heads_here, query_count), jnp.float32),
        jnp.zeros((heads_here, query_count, head_size), jnp.float32),
    )
    kv_all, clips_all = (
        lax.all_gather(kv_local, "ctx", axis=0, tiled=True),
        lax.all_gather(clip_of, "ctx", axis=0, tiled=True),
    )
    final = fold_keys(initial, kv_all, clips_all, queries, query_vis, score_scale)
    attended = (final[2] / final[1][:, :, None]).astype(jnp.bfloat16)
    attended_rows = jnp.transpose(attended, (1, 0, 2))
    return lax.psum_scatter(
        jnp.einsum(
            "rhd,hdo->ro", attended_rows, out_weight, preferred_element_type=jnp.float32
        ).astype(jnp.bfloat16),
        "head",
        scatter_dimension=0,
        tiled=True,
    )


def solution(mesh):
    placed = (
        P("ctx", None),
        P(None, None, "head", None),
        P("head", None, None),
        P(),
        P(),
        P("ctx"),
        P(),
    )
    return jax.shard_map(
        per_device, mesh=mesh, in_specs=placed, out_specs=P(("ctx", "head"), None), check_vma=False
    )
```

profile of v0, /device:TPU:1, one launch (start us, length us, event | category | flops | bytes accessed | tf_op | source)
XLA Modules:
  0.0 363.7 jit_solution(15202667989823776024)
XLA Ops:
  7.5 5.6 %fusion.20 = bf16[512,4096,1,1]{1,0,3,2:T(8,128)(2,1)S(1)} fusion(f32[16,4096]{1,0:T(8,128)S(1)} %copy-done, bf16[512,4096]{1,0:T(8,128)(2,1)} %param.9, s32[512]{0:T(512)S(1)} %select_reduce_fusion), kind=kOutput, calls=%fused_computation.29 | convolution fusion | flops 411049984 | bytes 8652800 | tf_op jit(solution)/shard_map/dot_general | solution.py:54
  13.1 10.1 %fusion.21 = bf16[512,3,4,128]{3,0,2,1:T(8,128)(2,1)S(1)} fusion(bf16[512,4096,1,1]{1,0,3,2:T(8,128)(2,1)S(1)} %fusion.20, bf16[4096,3,4,128]{3,2,1,0:T(4,128)(2,1)} %param.10), kind=kOutput, calls=%fused_computation.30 | convolution fusion | flops 6443237376 | bytes 18350080 | tf_op jit(solution)/shard_map/td,dchk->tchk/dot_general | solution.py:56
  23.2 1.1 slice.24
  24.4 26.2 %all-gather = s32[16,1,512]{2,1,0:T(1,128)S(1)} all-gather(s32[1,1,512]{2,1,0:T(1,128)S(1)} %bitcast.58), channel_id=1, replica_groups=mesh['ctx'=16,'head'=8] {'ctx'}, dimensions={0}, use_global_device_ids=true | all-gather | bytes 34816 | tf_op jit(solution)/shard_map/all_gather | solution.py:72
  51.1 86.8 %all-gather.3.cloned.1.call-done = bf16[8192,2,4,128]{3,0,2,1:T(8,128)(2,1)} async-done(((bf16[512,2,4,128]{3,0,2,1:T(8,128)(2,1)}), bf16[8192,2,4,128]{3,0,2,1:T(8,128)(2,1)}) %all-gather.3.cloned.1.call-update) | async-done | bytes 16777232 | tf_op jit(solution)/shard_map/all_gather | solution.py:71
  137.9 123.4 %while.18 = (s32[]{:T(128)}, f32[4,512]{1,0:T(4,128)S(1)}, f32[4,512]{1,0:T(4,128)S(1)}, f32[4,512,128]{2,1,0:T(8,128)}, s32[8192]{0:T(1024)S(1)}, /*index=5*/f3...) while((s32[]{:T(128)}, f32[4,512]{1,0:T(4,128)S(1)}, ...), condition=%wide.region_4.5_spmd.clone, body=%wide.region_1.4_spmd.clone.sunk | while | flops 752920576 | bytes 25958676 | solution.py:41
  138.7 2.0 fusion.46
  140.7 1.0 fusion.47
  141.8 2.9 fusion.49
  144.7 1.0 copy-done.4
  146.4 2.0 fusion.46
  148.4 1.0 fusion.47
  149.5 2.9 fusion.49
  152.4 1.0 copy-done.4
  154.1 2.0 fusion.46
  156.1 1.0 fusion.47
  157.2 2.9 fusion.49
  160.1 1.0 copy-done.4
  161.8 2.0 fusion.46
  163.8 1.0 fusion.47
  164.9 2.9 fusion.49
  167.8 1.0 copy-done.4
  169.5 2.0 fusion.46
  171.6 1.0 fusion.47
  172.6 2.9 fusion.49
  177.2 2.0 fusion.46
  179.3 1.0 fusion.47
  180.3 2.9 fusion.49
  184.9 2.0 fusion.46
  187.0 1.0 fusion.47
  188.1 2.9 fusion.49
  192.7 2.0 fusion.46
  194.7 1.0 fusion.47
  195.8 2.9 fusion.49
  198.7 1.0 copy-done.4
  200.4 2.0 fusion.46
  202.4 1.0 fusion.47
  203.5 2.9 fusion.49
  206.4 1.0 copy-done.4
  208.1 2.0 fusion.46
  210.1 1.0 fusion.47
  211.2 2.9 fusion.49
  215.8 2.0 fusion.46
  217.8 1.0 fusion.47
  218.9 2.9 fusion.49
  223.5 2.0 fusion.46
  225.5 1.0 fusion.47
  226.6 2.9 fusion.49
  231.2 2.0 fusion.46
  233.3 1.0 fusion.47
  234.3 2.9 fusion.49
  237.2 1.0 copy-done.4
  238.9 2.0 fusion.46
  241.0 1.0 fusion.47
  242.1 2.9 fusion.49
  244.9 1.0 copy-done.4
  246.7 2.0 fusion.46
  248.7 1.0 fusion.47
  249.8 2.9 fusion.49
  254.4 2.0 fusion.46
  256.4 1.0 fusion.47
  257.5 2.9 fusion.49
  261.3 6.9 %bitcast_convert_fusion = bf16[512,4096]{1,0:T(8,128)(2,1)} fusion(bf16[4,128,4096]{2,1,0:T(8,128)(2,1)} %param.11, f32[4,512,128]{2,1,0:T(8,128)} %get-tuple-element.145, f32[4,512]{1,0:T(4,128)S(1)} %get-tuple-element.146), kind=kOutput, calls=%fused_computation.27 | convolution fusion | flops 2150105088 | bytes 9445376 | tf_op jit(solution)/shard_map/rhd,hdo->ro/dot_general | solution.py:78
  268.2 88.6 %reduce-scatter.2.cloned.1.call-done = bf16[64,4096]{1,0:T(8,128)(2,1)} async-done(((bf16[512,4096]{1,0:T(8,128)(2,1)}), bf16[64,4096]{1,0:T(8,128)(2,1)}) %reduce-scatter.2.cloned.1.call-update) | async-done | bytes 524304 | tf_op jit(solution)/shard_map/reduce_scatter | solution.py:77
  (152 shorter events, 21.5 us)
Async XLA Ops:
  6.5 1.0 copy-start
  6.5 131.4 %all-gather.3.cloned.1.call-start = ((), (), s32[]{:S(2)}) async-start(), calls=%async_computation.1 | async-start | bytes 17825792 | tf_op jit(solution)/shard_map/all_gather | solution.py:71
  13.1 11.3 %copy-start.2 = (s32[512]{0:T(512)S(1)}, s32[512]{0:T(512)}, u32[]{:S(2)}) copy-start(s32[512]{0:T(512)} %param.14) | copy-start | bytes 6148
  13.1 37.5 %copy-start.1 = (s32[64,64]{1,0:T(8,128)S(1)}, s32[64,64]{1,0:T(8,128)}, u32[]{:S(2)}) copy-start(s32[64,64]{1,0:T(8,128)} %param.15) | copy-start | bytes 49156
  24.3 332.5 %reduce-scatter.2.cloned.1.call-start = ((), (), s32[]{:S(2)}) async-start(), calls=%async_computation.2 | async-start | bytes 4718592 | tf_op jit(solution)/shard_map/reduce_scatter | solution.py:77
  138.7 3.1 copy-start.3
  144.6 1.0 copy-start.4
  146.4 3.1 copy-start.3
  152.4 1.0 copy-start.4
  154.1 3.1 copy-start.3
  160.1 1.0 copy-start.4
  161.8 3.1 copy-start.3
  167.8 1.0 copy-start.4
  169.5 3.1 copy-start.3
  175.5 1.0 copy-start.4
  177.2 3.1 copy-start.3
  183.2 1.0 copy-start.4
  184.9 3.1 copy-start.3
  190.9 1.0 copy-start.4
  192.7 3.1 copy-start.3
  198.6 1.0 copy-start.4
  200.4 3.1 copy-start.3
  206.4 1.0 copy-start.4
  208.1 3.1 copy-start.3
  214.1 1.0 copy-start.4
  215.8 3.1 copy-start.3
  221.8 1.0 copy-start.4
  223.5 3.1 copy-start.3
  229.5 1.0 copy-start.4
  231.2 3.1 copy-start.3
  237.2 1.0 copy-start.4
  238.9 3.1 copy-start.3
  244.9 1.0 copy-start.4
  246.6 3.1 copy-start.3
  252.6 1.0 copy-start.4
  254.4 3.1 copy-start.3
  260.4 1.0 copy-start.4
Sparse Core Ops, SparseCore 0:
  24.5 113.4 all-gather.2
  268.3 88.4 reduce-scatter.1
where the time goes:
time: 365 us; the launch traced here: 364 us
  waiting for transfers between devices  175 us (48%)
  matrix products  112 us (31%)
  blocking collectives  26.2 us (7%)
  local copies, waits for them, and re-layouts  17.9 us (5%)
  other arithmetic  17.9 us (5%)
  between operations  13.5 us (4%)
    reduce_scatter x1, waiting for transfers between devices, per_device(): lax.psum_scatter(jnp.einsum('rhd,hdo->ro', attended_rows, out_weight, pre...  88.6 us
    all_gather x1, waiting for transfers between devices, per_device(): lax.all_gather(kv_local, 'ctx', axis=0, tiled=True)  86.8 us
    dot_general x16, matrix products, score_block(): jnp.einsum('hrk,khd->hrd', weights.astype(jnp.bfloat16), value_rows, pref...  45.8 us
    dot_general x16, matrix products, score_block(): jnp.einsum('rhd,khd->hrk', queries, key_rows, preferred_element_type=jnp....  32.2 us
    all_gather x1, blocking collectives, per_device(): lax.all_gather(clip_of, 'ctx', axis=0, tiled=True)  26.2 us
    reduce_sum x16, other arithmetic, score_block(): totals = totals * factor + jnp.sum(weights, axis=2)  16.6 us
    while x80, local copies, waits for them, and re-layouts  15.5 us
    dot_general x16, matrix products, score_block(): jnp.dot(query_vis, key_hot.T, precision=lax.Precision.HIGHEST) > 0.5  10.6 us
  transfers between devices with their start and end apart: 2, of which 2 were waited for; matrix products, arithmetic and copies ran while one was open for 0% of the time, Pallas kernels for 0%

commit v1 on v0

--- a/solution.py
+++ b/solution.py
@@ -3,6 +3,11 @@
 import jax.numpy as jnp
 from jax import lax
 from jax.sharding import PartitionSpec as P
+
+
+def all_by_exchange(x, mesh_axis, along):
+    repeated = jnp.stack([x] * lax.axis_size(mesh_axis))
+    return jnp.concatenate(lax.all_to_all(repeated, mesh_axis, 0, 0), axis=along)
 
 
 def score_block(state_now, kv_block, key_clips, queries, query_vis, score_scale):
@@ -69,7 +74,7 @@
     )
     kv_all, clips_all = (
         lax.all_gather(kv_local, "ctx", axis=0, tiled=True),
-        lax.all_gather(clip_of, "ctx", axis=0, tiled=True),
+        all_by_exchange(clip_of, "ctx", 0),
     )
     final = fold_keys(initial, kv_all, clips_all, queries, query_vis, score_scale)
     attended = (final[2] / final[1][:, :, None]).astype(jnp.bfloat16)

time: 365 us -> 348 us (0.953)
  blocking collectives: 26.2 us -> 0 us
  waiting for transfers between devices: 175 us -> 193 us
  local copies, waits for them, and re-layouts: 17.9 us -> 3.16 us
  starting transfers between devices: 0.04 us -> 8.48 us
    all_gather x1 -> x0, blocking collectives: 26.2 us -> none  [per_device(): lax.all_gather(clip_of, 'ctx', axis=0, tiled=True)]
    while x80 -> x16, local copies, waits for them, and re-layouts: 15.5 us -> 0.04 us
    all_gather x1, waiting for transfers between devices: 86.8 us -> 97.1 us  [per_device(): lax.all_gather(kv_local, 'ctx', axis=0, tiled=True)]
    all_to_all x0 -> x1, starting transfers between devices: none -> 8.44 us  [all_by_exchange(): lax.all_to_all(repeated, mesh_axis, 0, 0)]
    all_to_all x0 -> x1, waiting for transfers between devices: none -> 6.8 us  [all_by_exchange(): lax.all_to_all(repeated, mesh_axis, 0, 0)]
  transfers between devices with their start and end apart: 2 -> 3, of which waited for: 2 -> 3; matrix products, arithmetic and copies ran while one was open for 0% -> 0% of each run, Pallas kernels for 0% -> 0%
where the time goes in v1:
time: 348 us; the launch traced here: 346 us
  waiting for transfers between devices  193 us (55%)
  matrix products  110 us (32%)
  other arithmetic  17.9 us (5%)
  between operations  13.5 us (4%)
  starting transfers between devices  8.48 us (2%)
    all_gather x1, waiting for transfers between devices, per_device(): lax.all_gather(kv_local, 'ctx', axis=0, tiled=True)  97.1 us
    reduce_scatter x1, waiting for transfers between devices, per_device(): lax.psum_scatter(jnp.einsum('rhd,hdo->ro', attended_rows, out_weight, pre...  88.6 us
    dot_general x16, matrix products, score_block(): jnp.einsum('hrk,khd->hrd', weights.astype(jnp.bfloat16), value_rows, pref...  45.8 us
    dot_general x16, matrix products, score_block(): jnp.einsum('rhd,khd->hrk', queries, key_rows, preferred_element_type=jnp....  30.9 us
    reduce_sum x16, other arithmetic, score_block(): totals = totals * factor + jnp.sum(weights, axis=2)  16.6 us
    dot_general x16, matrix products, score_block(): jnp.dot(query_vis, key_hot.T, precision=lax.Precision.HIGHEST) > 0.5  10.6 us
    dot_general x1, matrix products, per_device(): jnp.einsum('td,dchk->tchk', moduled, qkv_weight, preferred_element_type=j...  10.1 us
    all_to_all x1, starting transfers between devices, all_by_exchange(): lax.all_to_all(repeated, mesh_axis, 0, 0)  8.44 us
  transfers between devices with their start and end apart: 3, of which 3 were waited for; matrix products, arithmetic and copies ran while one was open for 0% of the time, Pallas kernels for 0%

profile of v1, /device:TPU:1, one launch (start us, length us, event | category | flops | bytes accessed | tf_op | source)
XLA Modules:
  0.0 346.2 jit_solution(17344369749537850653)
XLA Ops:
  6.5 0.8 select_reduce_fusion
  7.5 5.6 %fusion.20 = bf16[512,4096,1,1]{1,0,3,2:T(8,128)(2,1)S(1)} fusion(f32[16,4096]{1,0:T(8,128)S(1)} %copy-done, bf16[512,4096]{1,0:T(8,128)(2,1)} %param.9, s32[512]{0:T(512)S(1)} %select_reduce_fusion), kind=kOutput, calls=%fused_computation.29 | convolution fusion | flops 411049984 | bytes 8652800 | tf_op jit(solution)/shard_map/dot_general | solution.py:59
  13.1 10.1 %fusion.21 = bf16[512,3,4,128]{3,0,2,1:T(8,128)(2,1)S(1)} fusion(bf16[512,4096,1,1]{1,0,3,2:T(8,128)(2,1)S(1)} %fusion.20, bf16[4096,3,4,128]{3,2,1,0:T(4,128)(2,1)} %param.10), kind=kOutput, calls=%fused_computation.30 | convolution fusion | flops 6443237376 | bytes 18350080 | tf_op jit(solution)/shard_map/td,dchk->tchk/dot_general | solution.py:61
  23.2 1.1 slice.24
  24.9 8.4 %all-to-all-start = ((s32[16,1,512]{2,1,0:T(1,128)}), s32[16,1,512]{2,1,0:T(1,128)S(1)}, u32[]{:S(2)}, u32[]{:S(2)}) async-start(s32[16,1,512]{2,1,0:T(1,128)} %stack.2), calls=%async_computation | async-start | bytes 65536 | tf_op jit(solution)/shard_map/all_to_all | solution.py:10
  33.9 6.8 %all-to-all-done = s32[16,1,512]{2,1,0:T(1,128)S(1)} async-done(((s32[16,1,512]{2,1,0:T(1,128)}), s32[16,1,512]{2,1,0:T(1,128)S(1)}, u32[]{:S(2)}, u32[]{:S(2)}) %all-to-all-start) | async-done | bytes 32800 | tf_op jit(solution)/shard_map/all_to_all | solution.py:10
  40.7 97.1 %all-gather.2.cloned.1.call-done = bf16[8192,2,4,128]{3,0,2,1:T(8,128)(2,1)} async-done(((bf16[512,2,4,128]{3,0,2,1:T(8,128)(2,1)}), bf16[8192,2,4,128]{3,0,2,1:T(8,128)(2,1)}) %all-gather.2.cloned.1.call-update) | async-done | bytes 16777232 | tf_op jit(solution)/shard_map/all_gather | solution.py:76
  137.8 106.7 %while.18 = (s32[]{:T(128)}, f32[4,512]{1,0:T(4,128)S(1)}, f32[4,512]{1,0:T(4,128)S(1)}, f32[4,512,128]{2,1,0:T(8,128)S(1)}, s32[8192]{0:T(1024)S(1)}, /*index=5...) while((s32[]{:T(128)}, f32[4,512]{1,0:T(4,128)S(1)}, ...), condition=%wide.region_4.5_spmd.clone, body=%wide.region_1.4_spmd.clone.sunk | while | flops 752920576 | bytes 17570012 | solution.py:46
  137.9 0.7 fusion.45
  138.5 1.9 fusion.46
  140.5 1.0 fusion.47
  141.5 2.9 fusion.49
  144.5 0.7 fusion.45
  145.2 1.9 fusion.46
  147.2 1.0 fusion.47
  148.2 2.9 fusion.49
  151.2 0.7 fusion.45
  151.9 1.9 fusion.46
  153.8 1.0 fusion.47
  154.9 2.9 fusion.49
  157.9 0.7 fusion.45
  158.5 1.9 fusion.46
  160.5 1.0 fusion.47
  161.6 2.9 fusion.49
  164.5 0.7 fusion.45
  165.2 1.9 fusion.46
  167.2 1.0 fusion.47
  168.2 2.9 fusion.49
  171.2 0.7 fusion.45
  171.9 1.9 fusion.46
  173.8 1.0 fusion.47
  174.9 2.9 fusion.49
  178.5 1.9 fusion.46
  180.5 1.0 fusion.47
  181.6 2.9 fusion.49
  185.2 1.9 fusion.46
  187.2 1.0 fusion.47
  188.2 2.9 fusion.49
  191.9 1.9 fusion.46
  193.8 1.0 fusion.47
  194.9 2.9 fusion.49
  198.6 1.9 fusion.46
  200.5 1.0 fusion.47
  201.6 2.9 fusion.49
  205.2 1.9 fusion.46
  207.2 1.0 fusion.47
  208.2 2.9 fusion.49
  211.9 1.9 fusion.46
  213.8 1.0 fusion.47
  214.9 2.9 fusion.49
  218.6 1.9 fusion.46
  220.5 1.0 fusion.47
  221.6 2.9 fusion.49
  225.2 1.9 fusion.46
  227.2 1.0 fusion.47
  228.3 2.9 fusion.49
  231.9 1.9 fusion.46
  233.9 1.0 fusion.47
  234.9 2.9 fusion.49
  238.6 1.9 fusion.46
  240.5 1.0 fusion.47
  241.6 2.9 fusion.49
  244.5 6.2 %bitcast_convert_fusion = bf16[512,4096]{1,0:T(8,128)(2,1)} fusion(bf16[4,128,4096]{2,1,0:T(8,128)(2,1)} %param.11, f32[4,512,128]{2,1,0:T(8,128)S(1)} %get-tuple-element.145, f32[4,512]{1,0:T(4,128)S(1)} %get-tuple-element.146), kind=kOutput, calls=%fused_computation.27 | convolution fusion | flops 2150105088 | bytes 9445376 | tf_op jit(solution)/shard_map/rhd,hdo->ro/dot_general | solution.py:83
  250.7 88.6 %reduce-scatter.2.cloned.1.call-done = bf16[64,4096]{1,0:T(8,128)(2,1)} async-done(((bf16[512,4096]{1,0:T(8,128)(2,1)}), bf16[64,4096]{1,0:T(8,128)(2,1)}) %reduce-scatter.2.cloned.1.call-update) | async-done | bytes 524304 | tf_op jit(solution)/shard_map/reduce_scatter | solution.py:82
  (90 shorter events, 9.6 us)
Async XLA Ops:
  6.5 1.0 copy-start
  6.5 131.2 %all-gather.2.cloned.1.call-start = ((), (), s32[]{:S(2)}) async-start(), calls=%async_computation.2 | async-start | bytes 17825792 | tf_op jit(solution)/shard_map/all_gather | solution.py:76
  13.1 11.2 %copy-start.2 = (s32[512]{0:T(512)S(1)}, s32[512]{0:T(512)}, u32[]{:S(2)}) copy-start(s32[512]{0:T(512)} %param.14) | copy-start | bytes 6148
  23.2 10.3 %copy-start.1 = (s32[64,64]{1,0:T(8,128)S(1)}, s32[64,64]{1,0:T(8,128)}, u32[]{:S(2)}) copy-start(s32[64,64]{1,0:T(8,128)} %param.15) | copy-start | bytes 49156
  24.9 15.8 %all-to-all-start = ((s32[16,1,512]{2,1,0:T(1,128)}), s32[16,1,512]{2,1,0:T(1,128)S(1)}, u32[]{:S(2)}, u32[]{:S(2)}) async-start(s32[16,1,512]{2,1,0:T(1,128)} %stack.2), calls=%async_computation | async-start | bytes 65536 | tf_op jit(solution)/shard_map/all_to_all | solution.py:10
  33.4 305.9 %reduce-scatter.2.cloned.1.call-start = ((), (), s32[]{:S(2)}) async-start(), calls=%async_computation.3 | async-start | bytes 4718592 | tf_op jit(solution)/shard_map/reduce_scatter | solution.py:82
Sparse Core Ops, SparseCore 0:
  24.4 113.3 all-gather.1
  250.8 88.4 reduce-scatter.1
